TPU v7x, 512 devices: a whole 4x4x16 slice. The times are simulated.
512 devices in a mesh: gx: 8 (over x, core), gy: 4 (over y), gz: 16 (over z).
Axes of the slice: x: 4, y: 4, z: 16, core: 2. Of those that a mesh axis runs over, the one named last changes fastest.
Arguments:
- multipoles: bfloat16 [289, 262144], P(None, ('gx', 'gy', 'gz')), may hold values from -6 to 6
- up_shift: bfloat16 [8, 289, 289], replicated, may hold values from -0.125 to 0.125
- down_shift: bfloat16 [8, 289, 289], replicated, may hold values from -0.375 to 0.375
- far_shift: bfloat16 [8, 289, 289], replicated, may hold values from -0.09375 to 0.09375
- send_list: int32 [8, 64, 64, 16], P('gx', ('gy', 'gz')), may hold values from 0 to 511
- leaf_src: int32 [16, 262144], P(None, ('gx', 'gy', 'gz')), may hold values from 0 to 1535
- leaf_kind: int32 [16, 262144], P(None, ('gx', 'gy', 'gz')), may hold values from 0 to 7
- coarse_src: int32 [8, 64], replicated, may hold values from 0 to 63
- coarse_kind: int32 [8, 64], replicated, may hold values from 0 to 7
Outputs:
- leaf_local: bfloat16 [289, 262144], P(None, ('gx', 'gy', 'gz'))
All inputs are finite; a program needn't handle non-finite values.
Results may differ from a plain program's by a relative error of at most 0.014.
Values may be sent and summed in bfloat16 or wider, within the bound.
No kernel may reach another device: no remote copies, remote signals or barrier semaphores. Data moves between devices by JAX's collectives and lax.ppermute only.
A program may use at most 128 MiB of HBM per device.

v0:
```python
import jax
import jax.numpy as jnp
from jax import lax
from jax.sharding import PartitionSpec as P

LOCAL_LEVELS = 3


def lift_level(children, up_shift):
    coefs = children.shape[0]
    count = children.shape[1] // 8
    child_stack = children.reshape(coefs, count, 8).transpose(2, 0, 1).reshape(8 * coefs, count)
    shift_table = up_shift.transpose(1, 0, 2).reshape(coefs, 8 * coefs)
    return jnp.dot(shift_table, child_stack, preferred_element_type=jnp.float32)


def lower_level(parent, down_shift):
    coefs = parent.shape[0]
    count = parent.shape[1]
    spread = jnp.dot(
        down_shift.reshape(8 * coefs, coefs), parent, preferred_element_type=jnp.float32
    )
    return spread.reshape(8, coefs, count).transpose(1, 2, 0).reshape(coefs, 8 * count)


def gather_columns(column_block, axes):
    group = lax.axis_size(axes)
    width = column_block.shape[1]
    spread = jnp.broadcast_to(column_block[:, None, :], (column_block.shape[0], group, width))
    spread = spread.reshape(column_block.shape[0], group * width)
    return lax.all_to_all(spread, axes, split_axis=1, concat_axis=1, tiled=True)


def on_device(
    multipoles,
    up_shift,
    down_shift,
    far_shift,
    send_list,
    leaf_src,
    leaf_kind,
    coarse_src,
    coarse_kind,
):
    coefs = multipoles.shape[0]
    kind_count = far_shift.shape[0]
    flat_index = lax.axis_index(("gx", "gy", "gz"))
    coarse_box = flat_index // 8
    octant = flat_index % 8
    peer_count = lax.axis_size(("gy", "gz"))
    slot_count = send_list.shape[3]
    send_order = send_list.reshape(peer_count * slot_count)
    outgoing = jnp.take(multipoles, send_order, axis=1)
    arrived = lax.all_to_all(outgoing, ("gy", "gz"), split_axis=1, concat_axis=1, tiled=True)
    upward = multipoles
    for level in range(LOCAL_LEVELS):
        upward = lift_level(upward, up_shift).astype(jnp.bfloat16)
    row_boxes = gather_columns(upward, "gz")
    row_multi = lift_level(row_boxes, up_shift).astype(jnp.bfloat16)
    coarse_multi = gather_columns(row_multi, ("gx", "gy"))
    coarse_cols = coarse_src[:, coarse_box]
    coarse_kinds = coarse_kind[:, coarse_box]
    list_len = coarse_cols.shape[0]
    coarse_picked = jnp.take(coarse_multi, coarse_cols, axis=1)
    stacked = (
        jnp.take(far_shift, coarse_kinds, axis=0)
        .transpose(1, 0, 2)
        .reshape(coefs, list_len * coefs)
    )
    column_vec = coarse_picked.transpose(1, 0).reshape(list_len * coefs, 1)
    coarse_local = jnp.dot(stacked, column_vec, preferred_element_type=jnp.float32).astype(
        jnp.bfloat16
    )
    downward = jnp.dot(down_shift[octant], coarse_local, preferred_element_type=jnp.float32).astype(
        jnp.bfloat16
    )
    for level in range(LOCAL_LEVELS - 1):
        downward = lower_level(downward, down_shift).astype(jnp.bfloat16)
    chain_part = lower_level(downward, down_shift)
    buffer = jnp.concatenate([multipoles, arrived], axis=1)
    leaf_count = leaf_src.shape[1]
    picked = jnp.take(buffer, leaf_src, axis=1)
    kind_range = jnp.arange(kind_count, dtype=jnp.int32)
    kind_hot = (leaf_kind[None, :, :] == kind_range[:, None, None]).astype(jnp.bfloat16)
    grouped = jnp.einsum("plt,klt->kpt", picked, kind_hot, preferred_element_type=jnp.float32)
    grouped = grouped.reshape(kind_count * coefs, leaf_count)
    upper_part = grouped.astype(jnp.bfloat16)
    lower_part = (grouped - upper_part.astype(jnp.float32)).astype(jnp.bfloat16)
    shift_table = far_shift.transpose(1, 0, 2).reshape(coefs, kind_count * coefs)
    far_total = jnp.dot(shift_table, upper_part, preferred_element_type=jnp.float32)
    far_total = far_total + jnp.dot(shift_table, lower_part, preferred_element_type=jnp.float32)
    return (chain_part + far_total).astype(jnp.bfloat16)


def solution(mesh):
    in_specs = (
        P(None, ("gx", "gy", "gz")),
        P(),
        P(),
        P(),
        P("gx", ("gy", "gz"), None, None),
        P(None, ("gx", "gy", "gz")),
        P(None, ("gx", "gy", "gz")),
        P(),
        P(),
    )
    out_specs = P(None, ("gx", "gy", "gz"))
    return jax.shard_map(
        on_device, mesh=mesh, in_specs=in_specs, out_specs=out_specs, check_vma=False
    )
```

profile of v0, /device:TPU:8, one launch (start us, length us, event | category | flops | bytes accessed | tf_op | source)
XLA Modules:
  0.0 159.2 jit_solution(3946871346502079837)
XLA Ops:
  0.0 1.2 copy.69
  1.2 0.0 copy-start.4
  1.2 4.2 %reshape.156 = bf16[289,2312]{1,0:T(8,128)(2,1)} reshape(bf16[289,8,289]{2,1,0:T(8,128)(2,1)} %bitcast.158) | data formatting | bytes 2672672 | tf_op jit(solution)/shard_map/reshape | solution.py:13
  5.4 0.0 copy-done.4
  5.4 0.7 fusion.39
  6.1 0.0 copy-start.10
  6.2 0.6 fusion.48
  6.7 0.1 reshape.200
  6.9 1.9 %convolution_reduce_fusion.1 = bf16[289]{0:T(512)(128)(2,1)S(1)} fusion(bf16[2312,1]{0,1:T(2,128)(2,1)S(1)} %reshape.200, bf16[289,2312]{1,0:T(8,128)(2,1)} %reshape.156), kind=kOutput, calls=%fused_computation.45 | convolution fusion | flops 1336336 | bytes 1341538 | tf_op jit(solution)/shard_map/dot_general | solution.py:14
  8.7 0.6 reshape.157
  9.4 15.2 %all-to-all-start = ((bf16[289,16,1]{0,2,1:T(2,128)(2,1)}), bf16[289,16,1]{0,2,1:T(2,128)(2,1)S(1)}, u32[]{:S(2)}, u32[]{:S(2)}) async-start(bf16[289,16,1]{0,2,1:T(2,128)(2,1)} %reshape.157), calls=%async_computation | async-start | bytes 49152 | tf_op jit(solution)/shard_map/all_to_all | solution.py:31
  24.6 0.0 copy-done.10
  24.6 0.1 copy.80
  24.7 0.1 reshape.163
  24.8 3.9 %gather_fusion.2 = bf16[1024,289]{1,0:T(8,128)(2,1)S(1)} fusion(bf16[289,512]{0,1:T(8,128)(2,1)S(1)} %copy.69, s32[1024]{0:T(1024)S(1)} %broadcast_clamp_fusion.1), kind=kCustom, calls=%fused_computation.2 | custom fusion | bytes 1187840 | tf_op jit(solution)/shard_map/jit(_take)/gather | solution.py:53
  28.7 0.1 copy.79
  28.8 0.0 copy-start.8
  28.8 1.1 broadcast_select_fusion
  29.9 7.2 %all-to-all-done = bf16[289,16,1]{0,2,1:T(2,128)(2,1)S(1)} async-done(((bf16[289,16,1]{0,2,1:T(2,128)(2,1)}), bf16[289,16,1]{0,2,1:T(2,128)(2,1)S(1)}, u32[]{:S(2)}, u32[]{:S(2)}) %all-to-all-start) | async-done | bytes 9280 | tf_op jit(solution)/shard_map/all_to_all | solution.py:31
  37.1 2.2 %fusion.60 = bf16[289,2]{0,1:T(2,128)(2,1)S(1)} fusion(bf16[289,8,289]{2,1,0:T(8,128)(2,1)} %bitcast.159, bf16[289,2,8]{0,2,1:T(8,128)(2,1)S(1)} %bitcast.168), kind=kOutput, calls=%fused_computation.46 | convolution fusion | flops 2673250 | bytes 1346740 | tf_op jit(solution)/shard_map/dot_general | solution.py:14
  39.3 0.7 broadcast_in_dim.57
  40.0 7.5 %all-to-all-start.1 = ((bf16[289,32,2]{0,2,1:T(2,128)(2,1)}), bf16[289,32,2]{0,2,1:T(2,128)(2,1)S(1)}, u32[]{:S(2)}, u32[]{:S(2)}) async-start(bf16[289,32,2]{0,2,1:T(2,128)(2,1)} %broadcast_in_dim.57), calls=%async_computation.1 | async-start | bytes 98304 | tf_op jit(solution)/shard_map/all_to_all | solution.py:31
  47.5 0.0 copy-done.8
  47.6 6.2 %all-to-all-done.1 = bf16[289,32,2]{0,2,1:T(2,128)(2,1)S(1)} async-done(((bf16[289,32,2]{0,2,1:T(2,128)(2,1)}), bf16[289,32,2]{0,2,1:T(2,128)(2,1)S(1)}, u32[]{:S(2)}, u32[]{:S(2)}) %all-to-all-start.1) | async-done | bytes 37024 | tf_op jit(solution)/shard_map/all_to_all | solution.py:31
  53.7 7.5 %all-to-all-start.2 = ((bf16[289,64,16]{0,2,1:T(8,128)(2,1)}), bf16[289,64,16]{0,2,1:T(8,128)(2,1)S(1)}, u32[]{:S(2)}, u32[]{:S(2)}) async-start(bf16[289,64,16]{0,2,1:T(8,128)(2,1)} %broadcast_select_fusion), calls=%async_computation.2 | async-start | bytes 1572864 | tf_op jit(solution)/shard_map/all_to_all | solution.py:54
  61.2 0.0 copy-done.3
  61.2 3.1 %copy.76 = bf16[8,289,289]{1,0,2:T(8,128)(2,1)} copy(bf16[8,289,289]{2,0,1:T(8,128)(2,1)S(1)} %copy-done.3) | data formatting | bytes 2672672 | tf_op args[2]
  64.4 4.2 %reshape.159 = bf16[2312,289]{0,1:T(8,128)(2,1)} reshape(bf16[8,289,289]{1,0,2:T(8,128)(2,1)} %copy.76) | data formatting | bytes 2672672 | tf_op jit(solution)/shard_map/reshape | solution.py:21
  68.6 0.0 copy-done.9
  68.6 0.8 copy.77
  69.5 0.2 copy.78
  69.7 0.0 copy-done.11
  69.7 0.2 fusion.74
  69.9 0.0 copy-done
  69.9 6.8 %gather_fusion = bf16[8,289,289]{2,0,1:T(8,128)(2,1)} fusion(bf16[8,289,289]{2,0,1:T(8,128)(2,1)S(1)} %copy-done, s32[1024]{0:T(1024)S(1)} %pad_clamp_fusion.1), kind=kCustom, calls=%fused_computation | custom fusion | bytes 2672704 | tf_op jit(solution)/shard_map/jit(_take)/gather | solution.py:66
  76.7 3.2 %copy.95 = bf16[289,8,289]{0,1,2:T(8,128)(2,1)} copy(bf16[289,8,289]{2,1,0:T(8,128)(2,1)S(1)} %bitcast.156) | data formatting | bytes 2672672 | tf_op jit(solution)/shard_map/transpose | solution.py:89
  79.8 0.0 copy-done.12
  79.8 0.2 fusion.75
  80.0 0.2 and_reduce_fusion
  80.3 1.9 %constant_dynamic-slice_fusion = bf16[1,289,289]{2,0,1:T(2,128)(2,1)S(1)} fusion(bf16[8,289,289]{2,0,1:T(8,128)(2,1)} %param.11, s32[]{:T(128)S(6)} %select_n.79), kind=kLoop, calls=%fused_computation.77 | loop fusion | bytes 334088 | tf_op jit(solution)/shard_map/dynamic_slice | solution.py:74
  82.2 3.0 %select_bitcast_fusion = bf16[289,8,289]{2,1,0:T(8,128)(2,1)} fusion(bf16[8,289,289]{2,0,1:T(8,128)(2,1)} %gather_fusion, pred[8]{0:T(512)(128)(4,1)S(1)} %get-tuple-element.6), kind=kLoop, calls=%fused_computation.21 | loop fusion | flops 668168 | bytes 2672680 | tf_op jit(solution)/shard_map/jit(_take)/select_n | solution.py:66
  85.3 0.6 gather_fusion.1
  85.9 0.1 select_bitcast_fusion.1
  85.9 2.2 %fusion.57 = bf16[289]{0:T(512)(128)(2,1)S(1)} fusion(bf16[289,8,289]{2,1,0:T(8,128)(2,1)} %select_bitcast_fusion, bf16[8,289,1]{1,0,2:T(8,128)(2,1)S(1)} %select_bitcast_fusion.1), kind=kOutput, calls=%fused_computation.43 | convolution fusion | flops 1336336 | bytes 1341538 | tf_op jit(solution)/shard_map/dot_general | solution.py:71
  88.2 0.2 convolution_reduce_fusion
  88.4 2.2 %fusion.8 = bf16[1,8,289]{2,0,1:T(2,128)(2,1)S(1)} fusion(bf16[289,1,1]{0,1,2:T(2,128)(2,1)S(1)} %reshape.207, bf16[8,289,289]{2,0,1:T(8,128)(2,1)} %param.11), kind=kOutput, calls=%fused_computation.17 | convolution fusion | flops 1336336 | bytes 1341538 | tf_op jit(solution)/shard_map/dot_general | solution.py:20
  90.5 0.0 copy-done.2
  90.5 0.3 fusion.4
  90.9 0.1 convert_element_type.85
  91.0 1.2 convolution_bitcast_fusion
  92.2 1.5 reshape.160
  93.7 1.1 copy.89
  94.8 8.9 %all-to-all-done.2 = bf16[289,64,16]{0,2,1:T(8,128)(2,1)S(1)} async-done(((bf16[289,64,16]{0,2,1:T(8,128)(2,1)}), bf16[289,64,16]{0,2,1:T(8,128)(2,1)S(1)}, u32[]{:S(2)}, u32[]{:S(2)}) %all-to-all-start.2) | async-done | bytes 591904 | tf_op jit(solution)/shard_map/all_to_all | solution.py:54
  103.8 0.1 pad_maximum_fusion
  103.9 0.0 copy-start.7
  103.9 33.2 %gather_fusion.3 = bf16[8192,289]{1,0:T(8,128)(2,1)} fusion(bf16[289,1536]{0,1:T(8,128)(2,1)S(1)} %pad_maximum_fusion, s32[8192]{0:T(1024)S(1)} %broadcast_clamp_fusion), kind=kCustom, calls=%fused_computation.3 | custom fusion | bytes 9502720 | tf_op jit(solution)/shard_map/jit(_take)/gather | solution.py:82
  137.1 0.0 copy-done.7
  137.1 10.0 %fusion = f32[512,8,289]{2,1,0:T(8,128)} fusion(bf16[16,512,289]{2,1,0:T(8,128)(2,1)} %bitcast.162, pred[16,512]{0,1:T(8,128)(4,1)S(1)} %copy.78, s32[16,512]{0,1:T(8,128)S(1)} %copy-done.7), kind=kOutput, calls=%fused_computation.4 | convolution fusion | flops 40312832 | bytes 9510912 | tf_op jit(solution)/shard_map/plt,klt->kpt/dot_general | solution.py:85
  147.1 6.5 %copy.84 = f32[512,8,289]{0,1,2:T(8,128)} copy(f32[512,8,289]{2,1,0:T(8,128)} %fusion) | data formatting | bytes 9469952 | tf_op jit(solution)/shard_map/plt,klt->kpt/dot_general | solution.py:85
  153.6 0.0 copy-done.5
  153.6 3.5 %convolution_bitcast_fusion.1 = f32[512,289]{0,1:T(8,128)S(1)} fusion(bf16[289,8,289]{0,1,2:T(8,128)(2,1)S(1)} %copy-done.5, f32[512,8,289]{0,1,2:T(8,128)} %copy.84), kind=kOutput, calls=%fused_computation.29 | convolution fusion | flops 684204032 | bytes 6663184 | tf_op jit(solution)/shard_map/dot_general | solution.py:90
  157.1 0.2 copy-done.1
  157.3 0.2 copy-done.6
  157.5 1.7 %fusion.30 = bf16[289,512]{1,0:T(8,128)(2,1)} fusion(f32[289,512]{1,0:T(8,128)S(1)} %copy-done.6, f32[512,289]{0,1:T(8,128)S(1)} %convolution_bitcast_fusion.1, bf16[289,8,289]{0,1,2:T(8,128)(2,1)S(1)} %copy-done.5, f32[512,8,289]{0,1,2:T(8,128)S(1)} %copy-done.1), kind=kOutput, calls=%fused_computation.33 | convolution fusion | flops 689382912 | bytes 7550992 | tf_op jit(solution)/shard_map/dot_general | solution.py:91
  (22 shorter events, 0.1 us)
Async XLA Ops:
  1.2 4.2 %copy-start.4 = (bf16[8,289,289]{2,0,1:T(8,128)(2,1)S(1)}, bf16[8,289,289]{2,0,1:T(8,128)(2,1)}, u32[]{:S(2)}) copy-start(bf16[8,289,289]{2,0,1:T(8,128)(2,1)} %param.10) | copy-start | bytes 4009012
  6.1 18.4 %copy-start.10 = (s32[1,1,64,16]{2,3,1,0:T(8,128)S(1)}, s32[1,1,64,16]{2,3,1,0:T(8,128)}, u32[]{:S(2)}) copy-start(s32[1,1,64,16]{2,3,1,0:T(8,128)} %param.13) | copy-start | bytes 12292
  9.4 27.8 %all-to-all-start = ((bf16[289,16,1]{0,2,1:T(2,128)(2,1)}), bf16[289,16,1]{0,2,1:T(2,128)(2,1)S(1)}, u32[]{:S(2)}, u32[]{:S(2)}) async-start(bf16[289,16,1]{0,2,1:T(2,128)(2,1)} %reshape.157), calls=%async_computation | async-start | bytes 49152 | tf_op jit(solution)/shard_map/all_to_all | solution.py:31
  28.8 18.7 %copy-start.8 = (s32[16,512]{1,0:T(8,128)S(1)}, s32[16,512]{1,0:T(8,128)}, u32[]{:S(2)}) copy-start(s32[16,512]{1,0:T(8,128)} %param.14) | copy-start | bytes 98308
  37.1 24.1 %copy-start.3 = (bf16[8,289,289]{2,0,1:T(8,128)(2,1)S(1)}, bf16[8,289,289]{2,0,1:T(8,128)(2,1)}, u32[]{:S(2)}) copy-start(bf16[8,289,289]{2,0,1:T(8,128)(2,1)} %param.11) | copy-start | bytes 4009012
  40.0 13.7 %all-to-all-start.1 = ((bf16[289,32,2]{0,2,1:T(2,128)(2,1)}), bf16[289,32,2]{0,2,1:T(2,128)(2,1)S(1)}, u32[]{:S(2)}, u32[]{:S(2)}) async-start(bf16[289,32,2]{0,2,1:T(2,128)(2,1)} %broadcast_in_dim.57), calls=%async_computation.1 | async-start | bytes 98304 | tf_op jit(solution)/shard_map/all_to_all | solution.py:31
  53.7 50.0 %all-to-all-start.2 = ((bf16[289,64,16]{0,2,1:T(8,128)(2,1)}), bf16[289,64,16]{0,2,1:T(8,128)(2,1)S(1)}, u32[]{:S(2)}, u32[]{:S(2)}) async-start(bf16[289,64,16]{0,2,1:T(8,128)(2,1)} %broadcast_select_fusion), calls=%async_computation.2 | async-start | bytes 1572864 | tf_op jit(solution)/shard_map/all_to_all | solution.py:54
  64.4 4.2 %copy-start.9 = (s32[16,512]{1,0:T(8,128)S(1)}, s32[16,512]{1,0:T(8,128)}, u32[]{:S(2)}) copy-start(s32[16,512]{1,0:T(8,128)} %param.15) | copy-start | bytes 98308
  64.4 5.3 %copy-start.11 = (s32[8,64]{1,0:T(8,128)S(1)}, s32[8,64]{1,0:T(8,128)}, u32[]{:S(2)}) copy-start(s32[8,64]{1,0:T(8,128)} %param.17) | copy-start | bytes 6148
  64.4 5.5 %copy-start = (bf16[8,289,289]{2,0,1:T(8,128)(2,1)S(1)}, bf16[8,289,289]{2,0,1:T(8,128)(2,1)}, u32[]{:S(2)}) copy-start(bf16[8,289,289]{2,0,1:T(8,128)(2,1)} %param.12) | copy-start | bytes 4009012
  76.7 3.2 %copy-start.12 = (s32[8,64]{1,0:T(8,128)S(1)}, s32[8,64]{1,0:T(8,128)}, u32[]{:S(2)}) copy-start(s32[8,64]{1,0:T(8,128)} %param.16) | copy-start | bytes 6148
  85.9 4.6 %copy-start.2 = (bf16[2312,289]{0,1:T(8,128)(2,1)S(1)}, bf16[2312,289]{0,1:T(8,128)(2,1)}, u32[]{:S(2)}) copy-start(bf16[2312,289]{0,1:T(8,128)(2,1)} %reshape.159) | copy-start | bytes 4009012
  103.9 33.2 %copy-start.7 = (s32[16,512]{0,1:T(8,128)S(1)}, s32[16,512]{0,1:T(8,128)}, u32[]{:S(2)}) copy-start(s32[16,512]{0,1:T(8,128)} %copy.77) | copy-start | bytes 98308
  147.0 6.5 %copy-start.5 = (bf16[289,8,289]{0,1,2:T(8,128)(2,1)S(1)}, bf16[289,8,289]{0,1,2:T(8,128)(2,1)}, u32[]{:S(2)}) copy-start(bf16[289,8,289]{0,1,2:T(8,128)(2,1)} %copy.95) | copy-start | bytes 4009012
  153.6 3.8 %copy-start.1 = (f32[512,8,289]{0,1,2:T(8,128)S(1)}, f32[512,8,289]{0,1,2:T(8,128)}, u32[]{:S(2)}) copy-start(f32[512,8,289]{0,1,2:T(8,128)} %copy.84) | copy-start | bytes 14204932
  153.6 3.9 %copy-start.6 = (f32[289,512]{1,0:T(8,128)S(1)}, f32[289,512]{1,0:T(8,128)}, u32[]{:S(2)}) copy-start(f32[289,512]{1,0:T(8,128)} %copy.89) | copy-start | bytes 1775620
where the time goes:
time: 160 us; the launch traced here: 159 us
  local copies, waits for them, and re-layouts  74.7 us (47%)
  starting transfers between devices  30.2 us (19%)
  matrix products  26.7 us (17%)
  waiting for transfers between devices  22.3 us (14%)
  other arithmetic  4.96 us (3%)
    gather x1, local copies, waits for them, and re-layouts, on_device(): picked = jnp.take(buffer, leaf_src, axis=1)  33.2 us
    all_to_all x2, starting transfers between devices, gather_columns(): return lax.all_to_all(spread, axes, split_axis=1, concat_axis=1, tiled=True)  22.7 us
    all_to_all x2, waiting for transfers between devices, gather_columns(): return lax.all_to_all(spread, axes, split_axis=1, concat_axis=1, tiled=True)  13.4 us
    dot_general x1, matrix products, on_device(): jnp.einsum('plt,klt->kpt', picked, kind_hot, preferred_element_type=jnp.f...  9.96 us
    all_to_all x1, waiting for transfers between devices, on_device(): lax.all_to_all(outgoing, ('gy', 'gz'), split_axis=1, concat_axis=1, tiled...  8.93 us
    all_to_all x1, starting transfers between devices, on_device(): lax.all_to_all(outgoing, ('gy', 'gz'), split_axis=1, concat_axis=1, tiled...  7.45 us
    gather x1, local copies, waits for them, and re-layouts, on_device(): jnp.take(far_shift, coarse_kinds, axis=0).transpose(1, 0, 2)  6.81 us
    dot_general x1, local copies, waits for them, and re-layouts, on_device(): jnp.einsum('plt,klt->kpt', picked, kind_hot, preferred_element_type=jnp.f...  6.5 us
  transfers between devices with their start and end apart: 3, of which 3 were waited for; matrix products, arithmetic and copies ran while one was open for 24% of the time, Pallas kernels for 0%

commit v1 on v0

--- a/solution.py
+++ b/solution.py
@@ -28,7 +28,15 @@
     width = column_block.shape[1]
     spread = jnp.broadcast_to(column_block[:, None, :], (column_block.shape[0], group, width))
     spread = spread.reshape(column_block.shape[0], group * width)
-    return lax.all_to_all(spread, axes, split_axis=1, concat_axis=1, tiled=True)
+    return jnp.concatenate(
+        lax.all_to_all(
+            jnp.stack(jnp.split(spread, lax.axis_size(axes), axis=1)),
+            axis_name=axes,
+            split_axis=0,
+            concat_axis=0,
+        ),
+        axis=1,
+    )
 
 
 def on_device(

time: 160 us -> 178 us (1.11)
  local copies, waits for them, and re-layouts: 74.7 us -> 93 us
    unnamed x32 -> x60, local copies, waits for them, and re-layouts: 5.69 us -> 24.9 us
    all_to_all x1, waiting for transfers between devices: 8.93 us -> 11.3 us  [on_device(): lax.all_to_all(outgoing, ('gy', 'gz'), split_axis=1, concat_axis=1, tiled...]
  transfers between devices with their start and end apart: 3 -> 3, of which waited for: 3 -> 3; matrix products, arithmetic and copies ran while one was open for 24% -> 21% of each run, Pallas kernels for 0% -> 0%
where the time goes in v1:
time: 178 us
  local copies, waits for them, and re-layouts  93 us (52%)
  starting transfers between devices  30.4 us (17%)
  matrix products  25.2 us (14%)
  waiting for transfers between devices  23.6 us (13%)
  other arithmetic  4.98 us (3%)
    gather x1, local copies, waits for them, and re-layouts, on_device(): picked = jnp.take(buffer, leaf_src, axis=1)  33.2 us
    unnamed x60, local copies, waits for them, and re-layouts  24.9 us
    all_to_all x2, starting transfers between devices, gather_columns(): lax.all_to_all(jnp.stack(jnp.split(spread, lax.axis_size(axes), axis=1)),...  22.7 us
    all_to_all x2, waiting for transfers between devices, gather_columns(): lax.all_to_all(jnp.stack(jnp.split(spread, lax.axis_size(axes), axis=1)),...  12.3 us
    all_to_all x1, waiting for transfers between devices, on_device(): lax.all_to_all(outgoing, ('gy', 'gz'), split_axis=1, concat_axis=1, tiled...  11.3 us
    dot_general x1, matrix products, on_device(): jnp.einsum('plt,klt->kpt', picked, kind_hot, preferred_element_type=jnp.f...  9.96 us
    all_to_all x1, starting transfers between devices, on_device(): lax.all_to_all(outgoing, ('gy', 'gz'), split_axis=1, concat_axis=1, tiled...  7.68 us
    gather x1, local copies, waits for them, and re-layouts, on_device(): jnp.take(far_shift, coarse_kinds, axis=0).transpose(1, 0, 2)  6.81 us
  transfers between devices with their start and end apart: 3, of which 3 were waited for; matrix products, arithmetic and copies ran while one was open for 21% of the time, Pallas kernels for 0%

profile of v1, /device:TPU:8, one launch (start us, length us, event | category | flops | bytes accessed | tf_op | source)
XLA Modules:
  0.0 177.5 jit_solution(18127823725737857489)
XLA Ops:
  0.0 1.2 copy.70
  1.2 4.2 %reshape.170 = bf16[289,2312]{1,0:T(8,128)(2,1)} reshape(bf16[289,8,289]{2,1,0:T(8,128)(2,1)} %bitcast.291) | data formatting | bytes 2672672 | tf_op jit(solution)/shard_map/reshape | solution.py:13
  5.4 0.7 fusion.39
  6.2 0.6 fusion.48
  6.9 1.9 %convolution_reduce_fusion.1 = bf16[289]{0:T(512)(128)(2,1)S(1)} fusion(bf16[2312,1]{0,1:T(2,128)(2,1)S(1)} %reshape.216, bf16[289,2312]{1,0:T(8,128)(2,1)} %reshape.170), kind=kOutput, calls=%fused_computation.45 | convolution fusion | flops 1336336 | bytes 1341538 | tf_op jit(solution)/shard_map/dot_general | solution.py:14
  8.7 0.6 stack.118
  9.4 15.2 %all-to-all-start = ((bf16[16,289,1]{1,2,0:T(2,128)(2,1)}), bf16[16,289,1]{1,2,0:T(2,128)(2,1)S(1)}, u32[]{:S(2)}, u32[]{:S(2)}) async-start(bf16[16,289,1]{1,2,0:T(2,128)(2,1)} %stack.118), calls=%async_computation | async-start | bytes 49152 | tf_op jit(solution)/shard_map/all_to_all | solution.py:32
  25.0 3.9 %gather_fusion.2 = bf16[1024,289]{1,0:T(8,128)(2,1)S(1)} fusion(bf16[289,512]{0,1:T(8,128)(2,1)S(1)} %copy.70, s32[1024]{0:T(1024)S(1)} %get-tuple-element.8), kind=kCustom, calls=%fused_computation.2 | custom fusion | bytes 1187840 | tf_op jit(solution)/shard_map/jit(_take)/gather | solution.py:61
  29.0 1.1 broadcast_select_fusion
  30.2 7.0 %all-to-all-done = bf16[16,289,1]{1,2,0:T(2,128)(2,1)S(1)} async-done(((bf16[16,289,1]{1,2,0:T(2,128)(2,1)}), bf16[16,289,1]{1,2,0:T(2,128)(2,1)S(1)}, u32[]{:S(2)}, u32[]{:S(2)}) %all-to-all-start) | async-done | bytes 9280 | tf_op jit(solution)/shard_map/all_to_all | solution.py:32
  37.2 2.2 %fusion.60 = bf16[289,2]{0,1:T(2,128)(2,1)S(1)} fusion(bf16[289,8,289]{2,1,0:T(8,128)(2,1)} %bitcast.292, bf16[289,2,8]{0,2,1:T(8,128)(2,1)S(1)} %bitcast.302), kind=kOutput, calls=%fused_computation.46 | convolution fusion | flops 2673250 | bytes 1346740 | tf_op jit(solution)/shard_map/dot_general | solution.py:14
  39.4 0.6 constant_dynamic-update-slice_fusion.31
  40.0 0.6 constant_dynamic-update-slice_fusion.30
  40.6 0.6 constant_dynamic-update-slice_fusion.29
  41.2 0.6 constant_dynamic-update-slice_fusion.28
  41.8 0.6 constant_dynamic-update-slice_fusion.27
  42.4 0.6 constant_dynamic-update-slice_fusion.26
  43.0 0.6 constant_dynamic-update-slice_fusion.25
  43.5 0.6 constant_dynamic-update-slice_fusion.24
  44.7 0.6 constant_dynamic-update-slice_fusion.22
  45.3 0.6 constant_dynamic-update-slice_fusion.21
  45.8 0.6 constant_dynamic-update-slice_fusion.20
  46.4 0.6 constant_dynamic-update-slice_fusion.19
  47.0 0.6 constant_dynamic-update-slice_fusion.18
  47.6 0.6 constant_dynamic-update-slice_fusion.17
  48.2 0.6 constant_dynamic-update-slice_fusion.16
  48.8 0.6 constant_dynamic-update-slice_fusion.15
  49.3 0.6 constant_dynamic-update-slice_fusion.14
  49.9 0.6 constant_dynamic-update-slice_fusion.13
  50.5 0.6 constant_dynamic-update-slice_fusion.12
  51.1 0.6 constant_dynamic-update-slice_fusion.11
  51.7 0.6 constant_dynamic-update-slice_fusion.10
  52.3 0.6 constant_dynamic-update-slice_fusion.9
  52.9 0.6 constant_dynamic-update-slice_fusion.8
  53.5 0.5 constant_dynamic-update-slice_fusion.7
  54.0 0.6 constant_dynamic-update-slice_fusion.6
  54.6 0.6 constant_dynamic-update-slice_fusion.5
  55.2 0.6 constant_dynamic-update-slice_fusion.4
  55.8 0.6 constant_dynamic-update-slice_fusion.3
  56.4 0.6 constant_dynamic-update-slice_fusion.2
  56.9 0.6 constant_dynamic-update-slice_fusion.1
  57.5 0.5 constant_dynamic-update-slice_fusion
  58.1 7.5 %all-to-all-start.1 = ((bf16[32,289,2]{1,2,0:T(2,128)(2,1)}), bf16[32,289,2]{1,2,0:T(2,128)(2,1)S(1)}, u32[]{:S(2)}, u32[]{:S(2)}) async-start(bf16[32,289,2]{1,2,0:T(2,128)(2,1)} %constant_dynamic-update-slice_fusion), calls=%async_computation.1 | async-start | bytes 98304 | tf_op jit(solution)/shard_map/all_to_all | solution.py:32
  65.7 0.8 copy.79
  66.5 5.3 %all-to-all-done.1 = bf16[32,289,2]{1,2,0:T(2,128)(2,1)S(1)} async-done(((bf16[32,289,2]{1,2,0:T(2,128)(2,1)}), bf16[32,289,2]{1,2,0:T(2,128)(2,1)S(1)}, u32[]{:S(2)}, u32[]{:S(2)}) %all-to-all-start.1) | async-done | bytes 37024 | tf_op jit(solution)/shard_map/all_to_all | solution.py:32
  71.8 7.7 %all-to-all-start.2 = ((bf16[289,64,16]{0,2,1:T(8,128)(2,1)}), bf16[289,64,16]{0,2,1:T(8,128)(2,1)S(1)}, u32[]{:S(2)}, u32[]{:S(2)}) async-start(bf16[289,64,16]{0,2,1:T(8,128)(2,1)} %broadcast_select_fusion), calls=%async_computation.2 | async-start | bytes 1572864 | tf_op jit(solution)/shard_map/all_to_all | solution.py:62
  79.7 3.2 %copy.97 = bf16[289,8,289]{0,1,2:T(8,128)(2,1)} copy(bf16[289,8,289]{2,1,0:T(8,128)(2,1)S(1)} %bitcast.289) | data formatting | bytes 2672672 | tf_op jit(solution)/shard_map/transpose | solution.py:97
  82.9 6.8 %gather_fusion = bf16[8,289,289]{2,0,1:T(8,128)(2,1)} fusion(bf16[8,289,289]{2,0,1:T(8,128)(2,1)S(1)} %copy-done, s32[1024]{0:T(1024)S(1)} %get-tuple-element.7), kind=kCustom, calls=%fused_computation | custom fusion | bytes 2672704 | tf_op jit(solution)/shard_map/jit(_take)/gather | solution.py:74
  89.7 4.2 %copy.78 = bf16[8,289,289]{1,0,2:T(8,128)(2,1)} copy(bf16[8,289,289]{2,0,1:T(8,128)(2,1)} %param.11) | data formatting | bytes 2672672 | tf_op args[2]
  93.9 3.3 %reshape.175 = bf16[2312,289]{0,1:T(8,128)(2,1)S(1)} reshape(bf16[8,289,289]{1,0,2:T(8,128)(2,1)} %copy.78) | data formatting | bytes 2672672 | tf_op jit(solution)/shard_map/reshape | solution.py:21
  97.6 1.9 %constant_dynamic-slice_fusion = bf16[1,289,289]{2,0,1:T(2,128)(2,1)S(1)} fusion(bf16[8,289,289]{2,0,1:T(8,128)(2,1)} %param.11, s32[]{:T(128)S(6)} %select_n.79), kind=kLoop, calls=%fused_computation.141 | loop fusion | bytes 334088 | tf_op jit(solution)/shard_map/dynamic_slice | solution.py:82
  99.6 3.0 %select_bitcast_fusion = bf16[289,8,289]{2,1,0:T(8,128)(2,1)} fusion(bf16[8,289,289]{2,0,1:T(8,128)(2,1)} %gather_fusion, pred[8]{0:T(512)(128)(4,1)S(1)} %get-tuple-element.6), kind=kLoop, calls=%fused_computation.21 | loop fusion | flops 668168 | bytes 2672680 | tf_op jit(solution)/shard_map/jit(_take)/select_n | solution.py:74
  102.7 0.6 gather_fusion.1
  103.3 2.2 %fusion.57 = bf16[289]{0:T(512)(128)(2,1)S(1)} fusion(bf16[289,8,289]{2,1,0:T(8,128)(2,1)} %select_bitcast_fusion, bf16[8,289,1]{1,0,2:T(8,128)(2,1)S(1)} %select_bitcast_fusion.1), kind=kOutput, calls=%fused_computation.43 | convolution fusion | flops 1336336 | bytes 1341538 | tf_op jit(solution)/shard_map/dot_general | solution.py:79
  105.8 0.7 fusion.8
  106.9 1.2 convolution_bitcast_fusion
  108.1 1.5 reshape.176
  109.7 1.1 copy.91
  110.7 11.3 %all-to-all-done.2 = bf16[289,64,16]{0,2,1:T(8,128)(2,1)S(1)} async-done(((bf16[289,64,16]{0,2,1:T(8,128)(2,1)}), bf16[289,64,16]{0,2,1:T(8,128)(2,1)S(1)}, u32[]{:S(2)}, u32[]{:S(2)}) %all-to-all-start.2) | async-done | bytes 591904 | tf_op jit(solution)/shard_map/all_to_all | solution.py:62
  122.2 33.2 %gather_fusion.3 = bf16[8192,289]{1,0:T(8,128)(2,1)} fusion(bf16[289,1536]{0,1:T(8,128)(2,1)S(1)} %pad_maximum_fusion, s32[8192]{0:T(1024)S(1)} %broadcast_clamp_fusion), kind=kCustom, calls=%fused_computation.3 | custom fusion | bytes 9502720 | tf_op jit(solution)/shard_map/jit(_take)/gather | solution.py:90
  155.4 10.0 %fusion = f32[512,8,289]{2,1,0:T(8,128)} fusion(bf16[16,512,289]{2,1,0:T(8,128)(2,1)} %bitcast.295, pred[16,512]{0,1:T(8,128)(4,1)S(1)} %copy.80, s32[16,512]{0,1:T(8,128)S(1)} %copy-done.6), kind=kOutput, calls=%fused_computation.4 | convolution fusion | flops 40312832 | bytes 9510912 | tf_op jit(solution)/shard_map/plt,klt->kpt/dot_general | solution.py:93
  165.4 6.5 %copy.86 = f32[512,8,289]{0,1,2:T(8,128)} copy(f32[512,8,289]{2,1,0:T(8,128)} %fusion) | data formatting | bytes 9469952 | tf_op jit(solution)/shard_map/plt,klt->kpt/dot_general | solution.py:93
  171.9 3.5 %convolution_bitcast_fusion.1 = f32[512,289]{0,1:T(8,128)S(1)} fusion(bf16[289,8,289]{0,1,2:T(8,128)(2,1)S(1)} %copy-done.4, f32[512,8,289]{0,1,2:T(8,128)} %copy.86), kind=kOutput, calls=%fused_computation.29 | convolution fusion | flops 684204032 | bytes 6663184 | tf_op jit(solution)/shard_map/dot_general | solution.py:98
  175.8 1.7 fusion.30
  (52 shorter events, 3.2 us)
Async XLA Ops:
  1.2 4.2 %copy-start.3 = (bf16[8,289,289]{2,0,1:T(8,128)(2,1)S(1)}, bf16[8,289,289]{2,0,1:T(8,128)(2,1)}, u32[]{:S(2)}) copy-start(bf16[8,289,289]{2,0,1:T(8,128)(2,1)} %param.10) | copy-start | bytes 4009012
  6.1 18.4 %copy-start.9 = (s32[1,1,64,16]{2,3,1,0:T(8,128)S(1)}, s32[1,1,64,16]{2,3,1,0:T(8,128)}, u32[]{:S(2)}) copy-start(s32[1,1,64,16]{2,3,1,0:T(8,128)} %param.13) | copy-start | bytes 12292
  6.2 18.6 %copy-start.10 = (s32[8,64]{1,0:T(8,128)S(1)}, s32[8,64]{1,0:T(8,128)}, u32[]{:S(2)}) copy-start(s32[8,64]{1,0:T(8,128)} %param.17) | copy-start | bytes 6148
  9.4 27.8 %all-to-all-start = ((bf16[16,289,1]{1,2,0:T(2,128)(2,1)}), bf16[16,289,1]{1,2,0:T(2,128)(2,1)S(1)}, u32[]{:S(2)}, u32[]{:S(2)}) async-start(bf16[16,289,1]{1,2,0:T(2,128)(2,1)} %stack.118), calls=%async_computation | async-start | bytes 49152 | tf_op jit(solution)/shard_map/all_to_all | solution.py:32
  29.0 36.6 %copy-start.7 = (s32[16,512]{1,0:T(8,128)S(1)}, s32[16,512]{1,0:T(8,128)}, u32[]{:S(2)}) copy-start(s32[16,512]{1,0:T(8,128)} %param.14) | copy-start | bytes 98308
  29.0 36.6 %copy-start.8 = (s32[16,512]{1,0:T(8,128)S(1)}, s32[16,512]{1,0:T(8,128)}, u32[]{:S(2)}) copy-start(s32[16,512]{1,0:T(8,128)} %param.15) | copy-start | bytes 98308
  37.2 42.5 %copy-start = (bf16[8,289,289]{2,0,1:T(8,128)(2,1)S(1)}, bf16[8,289,289]{2,0,1:T(8,128)(2,1)}, u32[]{:S(2)}) copy-start(bf16[8,289,289]{2,0,1:T(8,128)(2,1)} %param.12) | copy-start | bytes 4009012
  58.1 13.7 %all-to-all-start.1 = ((bf16[32,289,2]{1,2,0:T(2,128)(2,1)}), bf16[32,289,2]{1,2,0:T(2,128)(2,1)S(1)}, u32[]{:S(2)}, u32[]{:S(2)}) async-start(bf16[32,289,2]{1,2,0:T(2,128)(2,1)} %constant_dynamic-update-slice_fusion), calls=%async_computation.1 | async-start | bytes 98304 | tf_op jit(solution)/shard_map/all_to_all | solution.py:32
  71.8 50.3 %all-to-all-start.2 = ((bf16[289,64,16]{0,2,1:T(8,128)(2,1)}), bf16[289,64,16]{0,2,1:T(8,128)(2,1)S(1)}, u32[]{:S(2)}, u32[]{:S(2)}) async-start(bf16[289,64,16]{0,2,1:T(8,128)(2,1)} %broadcast_select_fusion), calls=%async_computation.2 | async-start | bytes 1572864 | tf_op jit(solution)/shard_map/all_to_all | solution.py:62
  93.9 3.3 %copy-start.11 = (s32[8,64]{1,0:T(8,128)S(1)}, s32[8,64]{1,0:T(8,128)}, u32[]{:S(2)}) copy-start(s32[8,64]{1,0:T(8,128)} %param.16) | copy-start | bytes 6148
  103.2 2.5 %copy-start.2 = (bf16[8,289,289]{2,0,1:T(8,128)(2,1)S(1)}, bf16[8,289,289]{2,0,1:T(8,128)(2,1)}, u32[]{:S(2)}) copy-start(bf16[8,289,289]{2,0,1:T(8,128)(2,1)} %param.11) | copy-start | bytes 4009012
  122.2 33.2 %copy-start.6 = (s32[16,512]{0,1:T(8,128)S(1)}, s32[16,512]{0,1:T(8,128)}, u32[]{:S(2)}) copy-start(s32[16,512]{0,1:T(8,128)} %copy.79) | copy-start | bytes 98308
  165.4 6.5 %copy-start.4 = (bf16[289,8,289]{0,1,2:T(8,128)(2,1)S(1)}, bf16[289,8,289]{0,1,2:T(8,128)(2,1)}, u32[]{:S(2)}) copy-start(bf16[289,8,289]{0,1,2:T(8,128)(2,1)} %copy.97) | copy-start | bytes 4009012
  171.9 3.8 %copy-start.1 = (f32[512,8,289]{0,1,2:T(8,128)S(1)}, f32[512,8,289]{0,1,2:T(8,128)}, u32[]{:S(2)}) copy-start(f32[512,8,289]{0,1,2:T(8,128)} %copy.86) | copy-start | bytes 14204932
  171.9 3.9 %copy-start.5 = (f32[289,512]{1,0:T(8,128)S(1)}, f32[289,512]{1,0:T(8,128)}, u32[]{:S(2)}) copy-start(f32[289,512]{1,0:T(8,128)} %copy.91) | copy-start | bytes 1775620
